TPU v7x, 256 devices: a whole 4x4x8 slice. The times are simulated.
256 devices in a mesh: gx: 16 (over z, x_hi), gy: 16 (over x_lo, y, core).
Axes of the slice: x: 4 (x_hi: 2, x_lo: 2; x = x_hi * 2 + x_lo), y: 4, z: 8, core: 2. Of those that a mesh axis runs over, the one named last changes fastest.
Arguments:
- adjoint_electric: float32 [3, 32, 2048, 512], P(None, 'gx', 'gy'), may hold values from -6 to 6
- adjoint_magnetic: float32 [3, 32, 2048, 512], P(None, 'gx', 'gy'), may hold values from -6 to 6
- second_electric: float32 [3, 32, 2048, 512], P(None, 'gx', 'gy'), may hold values from -6 to 6
- second_magnetic: float32 [3, 32, 2048, 512], P(None, 'gx', 'gy'), may hold values from -6 to 6
- saved_forward: bfloat16 [2, 3, 32, 2048, 512], P(None, None, 'gx', 'gy'), may hold values from -6 to 6
- saved_tangent: bfloat16 [2, 3, 32, 2048, 512], P(None, None, 'gx', 'gy'), may hold values from -6 to 6
- direction: float32 [32, 2048, 512], P('gx', 'gy'), may hold values from -6 to 6
- material: int32 [32, 2048, 512], P('gx', 'gy'), may hold values from 0 to 2
- source_mask: int32 [32, 2048, 512], P('gx', 'gy'), may hold values 0 or 1
Outputs:
- curvature: float32 [32, 2048, 512], P('gx', 'gy')
- updated_electric: float32 [3, 32, 2048, 512], P(None, 'gx', 'gy')
- updated_magnetic: float32 [3, 32, 2048, 512], P(None, 'gx', 'gy')
Inputs may be any that keep to these rules, and one draw needn't show every extreme that they name: material 0 is absorber, 1 capping, 2 vacuum.
All inputs are finite; a program needn't handle non-finite values. No bound on the sum of `source_mask` on one device may be relied on, other than what follows from the above.
Results may differ from a plain program's by a relative error of at most 0.00045.
Values sent between devices are 32-bit elements; how exact they have to be, the bound alone decides.
No kernel may reach another device: no remote copies, remote signals or barrier semaphores. Data moves between devices by JAX's collectives and lax.ppermute only.
A program may use at most 192 MiB of HBM per device.

v0:
```python
import jax
import jax.numpy as jnp
from jax import lax
from jax.sharding import PartitionSpec as P


TIME_STEP = 0.5


def from_behind(block, axis, distance):
    devices = range(lax.axis_size(axis))
    route = [((i - distance) % len(devices), i) for i in devices]
    return lax.ppermute(block, axis, route)


def back_y(f, row):
    return f - jnp.concatenate([row[None], f[:-1]], axis=0)


def back_z(f):
    return f - jnp.pad(f[:, :-1], ((0, 0), (1, 0)))


def ahead_y(f, row):
    return jnp.concatenate([f[1:], row[None]], axis=0) - f


def ahead_z(f):
    return jnp.pad(f[:, 1:], ((0, 0), (0, 1))) - f


def magnetic_plane(h, w, prev, rows):
    bx2 = w[2] if prev is None else w[2] - prev[2]
    bx1 = w[1] if prev is None else w[1] - prev[1]
    return jnp.stack(
        [
            h[0] + TIME_STEP * (back_y(w[2], rows[1]) - back_z(w[1])),
            h[1] + TIME_STEP * (back_z(w[0]) - bx2),
            h[2] + TIME_STEP * (bx1 - back_y(w[0], rows[0])),
        ]
    )


def electric_plane(e, h, nxt, rows, add):
    return jnp.stack(
        [
            e[0] - TIME_STEP * (ahead_y(h[2], rows[1]) - ahead_z(h[1])) + add[0],
            e[1] - TIME_STEP * (ahead_z(h[0]) - (nxt[1] - h[2])) + add[1],
            e[2] - TIME_STEP * ((nxt[0] - h[1]) - ahead_y(h[0], rows[0])) + add[2],
        ]
    )


def local(
    adjoint_electric,
    adjoint_magnetic,
    second_electric,
    second_magnetic,
    saved_forward,
    saved_tangent,
    direction,
    material,
    source_mask,
):
    planes = adjoint_electric.shape[1]
    permittivity = jnp.where(
        material == 0,
        jnp.float32(2.6),
        jnp.where(material == 1, jnp.float32(1.8), jnp.float32(1.0)),
    )
    coefficient = TIME_STEP / permittivity
    slope = -TIME_STEP * direction / (permittivity * permittivity)
    source = source_mask.astype(jnp.float32)
    first_weight = TIME_STEP / (permittivity * permittivity)
    second_weight = 2.0 * TIME_STEP * direction / (permittivity * permittivity * permittivity)

    ea = [adjoint_electric[:, p] for p in range(planes)]
    ha = [adjoint_magnetic[:, p] for p in range(planes)]
    es = [second_electric[:, p] for p in range(planes)]
    hs = [second_magnetic[:, p] for p in range(planes)]
    coef = [coefficient[p] for p in range(planes)]
    slo = [slope[p] for p in range(planes)]
    src = [source[p] for p in range(planes)]
    fw1 = [first_weight[p] for p in range(planes)]
    fw2 = [second_weight[p] for p in range(planes)]
    curvature = [None] * planes

    total_steps = saved_forward.shape[0]
    for section in reversed(range(total_steps)):
      forward = [saved_forward[section][:, p].astype(jnp.float32) for p in range(planes)]
      tangent = [saved_tangent[section][:, p].astype(jnp.float32) for p in range(planes)]
      wa = [coef[p] * ea[p] for p in range(planes)]
      ws = [coef[p] * es[p] + slo[p] * ea[p] for p in range(planes)]
      last = planes - 1
      edge_x = jnp.stack([wa[last][1], wa[last][2], ws[last][1], ws[last][2]])
      before_x = from_behind(edge_x, "gx", 1)
      edge_y = jnp.stack([jnp.stack([wa[p][0, -1], wa[p][2, -1], ws[p][0, -1], ws[p][2, -1]]) for p in range(planes)])
      before_y = from_behind(edge_y, "gy", 1)

      ha_new = [None] * planes
      hs_new = [None] * planes
      ha_new[0] = magnetic_plane(ha[0], wa[0], None, before_y[0, 0:2])
      hs_new[0] = magnetic_plane(hs[0], ws[0], None, before_y[0, 2:4])
      front_x = jnp.stack([ha_new[0][1], ha_new[0][2], hs_new[0][1], hs_new[0][2]])
      ha_new[0], hs_new[0], front_x = lax.optimization_barrier((ha_new[0], hs_new[0], front_x))
      after_x = from_behind(front_x, "gx", -1)
      for p in range(1, planes):
          ha_new[p] = magnetic_plane(ha[p], wa[p], wa[p - 1], before_y[p, 0:2])
          hs_new[p] = magnetic_plane(hs[p], ws[p], ws[p - 1], before_y[p, 2:4])
      ha_new[0] = jnp.stack(
          [ha_new[0][0], ha_new[0][1] + TIME_STEP * before_x[1], ha_new[0][2] - TIME_STEP * before_x[0]]
      )
      hs_new[0] = jnp.stack(
          [hs_new[0][0], hs_new[0][1] + TIME_STEP * before_x[3], hs_new[0][2] - TIME_STEP * before_x[2]]
      )
      ha, hs = ha_new, hs_new
      front_y = jnp.stack(
          [jnp.stack([ha[p][0, 0], ha[p][2, 0], hs[p][0, 0], hs[p][2, 0]]) for p in range(planes)]
      )
      after_y = from_behind(front_y, "gy", -1)
      right_a = jnp.stack([after_x[0] + TIME_STEP * edge_x[1], after_x[1] - TIME_STEP * edge_x[0]])
      right_s = jnp.stack([after_x[2] + TIME_STEP * edge_x[3], after_x[3] - TIME_STEP * edge_x[2]])

      ea_new = [None] * planes
      es_new = [None] * planes
      for p in range(planes):
          nxt_a = right_a if p == last else ha[p + 1][1:3]
          nxt_s = right_s if p == last else hs[p + 1][1:3]
          ea_new[p] = electric_plane(ea[p], ha[p], nxt_a, after_y[p, 0:2], src[p] * forward[p])
          es_new[p] = electric_plane(es[p], hs[p], nxt_s, after_y[p, 2:4], src[p] * tangent[p])
      ea, es = ea_new, es_new
      for p in range(planes):
          term = -fw1[p] * jnp.sum(tangent[p] * ea[p] + forward[p] * es[p], axis=0) + fw2[p] * jnp.sum(
              forward[p] * ea[p], axis=0
          )
          curvature[p] = term if curvature[p] is None else curvature[p] + term
    return (
        jnp.stack(curvature),
        jnp.stack(es, axis=1),
        jnp.stack(hs, axis=1),
    )


def solution(mesh):
    in_specs = (
        P(None, "gx", "gy", None),
        P(None, "gx", "gy", None),
        P(None, "gx", "gy", None),
        P(None, "gx", "gy", None),
        P(None, None, "gx", "gy", None),
        P(None, None, "gx", "gy", None),
        P("gx", "gy", None),
        P("gx", "gy", None),
        P("gx", "gy", None),
    )
    out_specs = (P("gx", "gy", None), P(None, "gx", "gy", None), P(None, "gx", "gy", None))
    return jax.shard_map(local, mesh=mesh, in_specs=in_specs, out_specs=out_specs, check_vma=False)
```

profile of v0, /device:TPU:25, one launch (start us, length us, event | category | flops | bytes accessed | tf_op | source)
XLA Modules:
  0.0 132.4 jit_solution(14068175988493591842)
XLA Ops:
  0.6 1.3 %multiply_divide_fusion.1 = (f32[2,128,512]{2,1,0:T(8,128)S(1)}, pred[2,128,512]{2,1,0:T(8,128)(4,1)S(1)}, pred[2,128,512]{2,1,0:T(8,128)(4,1)S(1)}) fusion(s32[2,128,512]{2,1,0:T(8,128)} %param.16), kind=kLoop, calls=%fused_computation.68 | loop fusion | flops 786432 | bytes 1310720 | tf_op jit(solution)/shard_map/div | solution.py:74
  2.4 1.0 copy-done.1
  3.4 0.5 copy-done
  3.9 0.5 fusion.13
  4.6 1.5 %collective-permute-start = (f32[2,4,512]{2,1,0:T(4,128)S(1)}, f32[2,4,512]{2,1,0:T(4,128)S(1)}, u32[]{:S(2)}, u32[]{:S(2)}) collective-permute-start(f32[2,4,512]{2,1,0:T(4,128)S(1)} %pad_maximum_fusion.19), channel_id=1, source_target_pairs={{15,0},{0,1},{1,2},{2,3},{3,4},{4,5},{5,6},{6,7},{7,8},{8,9},{9,10... | collective-permute-start | bytes 49160 | tf_op jit(solution)/shard_map/ppermute | solution.py:13
  6.3 2.5 %collective-permute-start.1 = (f32[4,128,512]{2,1,0:T(8,128)S(1)}, f32[4,128,512]{2,1,0:T(8,128)S(1)}, u32[]{:S(2)}, u32[]{:S(2)}) collective-permute-start(f32[4,128,512]{2,1,0:T(8,128)S(1)} %pad_maximum_fusion.3), channel_id=1, source_target_pairs={{240,0},{0,16},{16,32},{32,48},{48,64},{64,80},{80,96},{96,112},{1... | collective-permute-start | bytes 3145736 | tf_op jit(solution)/shard_map/ppermute | solution.py:13
  9.1 1.3 copy-done.5
  10.6 0.9 copy-done.6
  11.9 0.9 convert_multiply_fusion.5
  13.8 1.1 copy-done.3
  15.9 6.5 %collective-permute-start.3 = (f32[4,128,512]{2,1,0:T(8,128)S(1)}, f32[4,128,512]{2,1,0:T(8,128)S(1)}, u32[]{:S(2)}, u32[]{:S(2)}) collective-permute-start(f32[4,128,512]{2,1,0:T(8,128)S(1)} %pad_maximum_fusion.2), channel_id=1, source_target_pairs={{16,0},{32,16},{48,32},{64,48},{80,64},{96,80},{112,96},{128,112},... | collective-permute-start | bytes 3145736 | tf_op jit(solution)/shard_map/ppermute | solution.py:13
  22.4 31.8 %collective-permute-done.1 = f32[4,128,512]{2,1,0:T(8,128)S(1)} collective-permute-done((f32[4,128,512]{2,1,0:T(8,128)S(1)}, f32[4,128,512]{2,1,0:T(8,128)S(1)}, u32[]{:S(2)}, u32[]{:S(2)}) %collective-permute-start.1) | collective-permute-done | bytes 1048608 | tf_op jit(solution)/shard_map/ppermute | solution.py:13
  54.2 0.5 fusion.99
  54.7 0.5 fusion.94
  55.2 0.7 collective-permute-start.2
  56.4 4.4 %collective-permute-done.2 = f32[2,4,512]{2,1,0:T(4,128)S(1)} collective-permute-done((f32[2,4,512]{2,1,0:T(4,128)S(1)}, f32[2,4,512]{2,1,0:T(4,128)S(1)}, u32[]{:S(2)}, u32[]{:S(2)}) %collective-permute-start.2) | collective-permute-done | bytes 16416 | tf_op jit(solution)/shard_map/ppermute | solution.py:13
  61.3 0.5 fusion.80
  61.9 0.4 fusion.98
  62.3 0.6 fusion.73
  64.7 0.6 fusion.1
  65.5 3.8 %collective-permute-start.5 = (f32[4,128,512]{2,1,0:T(8,128)S(1)}, f32[4,128,512]{2,1,0:T(8,128)S(1)}, u32[]{:S(2)}, u32[]{:S(2)}) collective-permute-start(f32[4,128,512]{2,1,0:T(8,128)S(1)} %pad_maximum_fusion.5), channel_id=1, source_target_pairs={{240,0},{0,16},{16,32},{32,48},{48,64},{64,80},{80,96},{96,112},{1... | collective-permute-start | bytes 3145736 | tf_op jit(solution)/shard_map/ppermute | solution.py:13
  70.4 6.4 %collective-permute-start.7 = (f32[4,128,512]{2,1,0:T(8,128)S(1)}, f32[4,128,512]{2,1,0:T(8,128)S(1)}, u32[]{:S(2)}, u32[]{:S(2)}) collective-permute-start(f32[4,128,512]{2,1,0:T(8,128)S(1)} %pad_maximum_fusion.4), channel_id=1, source_target_pairs={{16,0},{32,16},{48,32},{64,48},{80,64},{96,80},{112,96},{128,112},... | collective-permute-start | bytes 3145736 | tf_op jit(solution)/shard_map/ppermute | solution.py:13
  77.8 40.6 %collective-permute-done.7 = f32[4,128,512]{2,1,0:T(8,128)S(1)} collective-permute-done((f32[4,128,512]{2,1,0:T(8,128)S(1)}, f32[4,128,512]{2,1,0:T(8,128)S(1)}, u32[]{:S(2)}, u32[]{:S(2)}) %collective-permute-start.7) | collective-permute-done | bytes 1048608 | tf_op jit(solution)/shard_map/ppermute | solution.py:13
  118.7 0.6 fusion.60
  119.4 1.9 %collective-permute-start.6 = (f32[2,4,512]{2,1,0:T(4,128)S(1)}, f32[2,4,512]{2,1,0:T(4,128)S(1)}, u32[]{:S(2)}, u32[]{:S(2)}) collective-permute-start(f32[2,4,512]{2,1,0:T(4,128)S(1)} %pad_maximum_fusion.22), channel_id=1, source_target_pairs={{1,0},{2,1},{3,2},{4,3},{5,4},{6,5},{7,6},{8,7},{9,8},{10,9},{11,1... | collective-permute-start | bytes 49160 | tf_op jit(solution)/shard_map/ppermute | solution.py:13
  121.7 3.3 %collective-permute-done.6 = f32[2,4,512]{2,1,0:T(4,128)S(1)} collective-permute-done((f32[2,4,512]{2,1,0:T(4,128)S(1)}, f32[2,4,512]{2,1,0:T(4,128)S(1)}, u32[]{:S(2)}, u32[]{:S(2)}) %collective-permute-start.6) | collective-permute-done | bytes 16416 | tf_op jit(solution)/shard_map/ppermute | solution.py:13
  126.0 0.5 fusion.51
  127.9 0.6 fusion.3
  128.6 1.3 copy.21
  129.9 1.3 pad_maximum_fusion.1
  131.2 0.4 fusion.206
  131.5 0.8 pad_maximum_fusion.18
  (150 shorter events, 11.4 us)
Async XLA Ops:
  0.6 1.3 %copy-start.7 = (f32[2,128,512]{2,1,0:T(8,128)S(1)}, f32[2,128,512]{2,1,0:T(8,128)}, u32[]{:S(2)}) copy-start(f32[2,128,512]{2,1,0:T(8,128)} %param.15) | copy-start | bytes 1572868
  2.0 1.4 %copy-start.1 = (f32[3,2,128,512]{3,2,1,0:T(8,128)S(1)}, f32[3,2,128,512]{3,2,1,0:T(8,128)}, u32[]{:S(2)}) copy-start(f32[3,2,128,512]{3,2,1,0:T(8,128)} %param.11) | copy-start | bytes 4718596
  2.3 1.7 %copy-start = (f32[3,2,128,512]{3,2,1,0:T(8,128)S(1)}, f32[3,2,128,512]{3,2,1,0:T(8,128)}, u32[]{:S(2)}) copy-start(f32[3,2,128,512]{3,2,1,0:T(8,128)} %param.9) | copy-start | bytes 4718596
  4.6 8.3 %collective-permute-start = (f32[2,4,512]{2,1,0:T(4,128)S(1)}, f32[2,4,512]{2,1,0:T(4,128)S(1)}, u32[]{:S(2)}, u32[]{:S(2)}) collective-permute-start(f32[2,4,512]{2,1,0:T(4,128)S(1)} %pad_maximum_fusion.19), channel_id=1, source_target_pairs={{15,0},{0,1},{1,2},{2,3},{3,4},{4,5},{5,6},{6,7},{7,8},{8,9},{9,10... | collective-permute-start | bytes 49160 | tf_op jit(solution)/shard_map/ppermute | solution.py:13
  6.2 2.8 %copy-start.4 = (bf16[2,3,2,128,512]{4,3,2,1,0:T(8,128)(2,1)S(1)}, bf16[2,3,2,128,512]{4,3,2,1,0:T(8,128)(2,1)}, u32[]{:S(2)}) copy-start(bf16[2,3,2,128,512]{4,3,2,1,0:T(8,128)(2,1)} %param.13) | copy-start | bytes 4718596
  6.3 48.0 %collective-permute-start.1 = (f32[4,128,512]{2,1,0:T(8,128)S(1)}, f32[4,128,512]{2,1,0:T(8,128)S(1)}, u32[]{:S(2)}, u32[]{:S(2)}) collective-permute-start(f32[4,128,512]{2,1,0:T(8,128)S(1)} %pad_maximum_fusion.3), channel_id=1, source_target_pairs={{240,0},{0,16},{16,32},{32,48},{48,64},{64,80},{80,96},{96,112},{1... | collective-permute-start | bytes 3145736 | tf_op jit(solution)/shard_map/ppermute | solution.py:13
  9.0 1.4 %copy-start.5 = (bf16[2,3,2,128,512]{4,3,2,1,0:T(8,128)(2,1)S(1)}, bf16[2,3,2,128,512]{4,3,2,1,0:T(8,128)(2,1)}, u32[]{:S(2)}) copy-start(bf16[2,3,2,128,512]{4,3,2,1,0:T(8,128)(2,1)} %param.14) | copy-start | bytes 4718596
  10.4 1.0 copy-start.6
  11.9 1.4 %copy-start.2 = (f32[3,2,128,512]{3,2,1,0:T(8,128)S(1)}, f32[3,2,128,512]{3,2,1,0:T(8,128)}, u32[]{:S(2)}) copy-start(f32[3,2,128,512]{3,2,1,0:T(8,128)} %param.12) | copy-start | bytes 4718596
  13.5 1.4 %copy-start.3 = (f32[3,2,128,512]{3,2,1,0:T(8,128)S(1)}, f32[3,2,128,512]{3,2,1,0:T(8,128)}, u32[]{:S(2)}) copy-start(f32[3,2,128,512]{3,2,1,0:T(8,128)} %param.10) | copy-start | bytes 4718596
  15.9 45.4 %collective-permute-start.3 = (f32[4,128,512]{2,1,0:T(8,128)S(1)}, f32[4,128,512]{2,1,0:T(8,128)S(1)}, u32[]{:S(2)}, u32[]{:S(2)}) collective-permute-start(f32[4,128,512]{2,1,0:T(8,128)S(1)} %pad_maximum_fusion.2), channel_id=1, source_target_pairs={{16,0},{32,16},{48,32},{64,48},{80,64},{96,80},{112,96},{128,112},... | collective-permute-start | bytes 3145736 | tf_op jit(solution)/shard_map/ppermute | solution.py:13
  55.2 5.5 %collective-permute-start.2 = (f32[2,4,512]{2,1,0:T(4,128)S(1)}, f32[2,4,512]{2,1,0:T(4,128)S(1)}, u32[]{:S(2)}, u32[]{:S(2)}) collective-permute-start(f32[2,4,512]{2,1,0:T(4,128)S(1)} %pad_maximum_fusion.20), channel_id=1, source_target_pairs={{1,0},{2,1},{3,2},{4,3},{5,4},{6,5},{7,6},{8,7},{9,8},{10,9},{11,1... | collective-permute-start | bytes 49160 | tf_op jit(solution)/shard_map/ppermute | solution.py:13
  65.3 4.0 %collective-permute-start.4 = (f32[2,4,512]{2,1,0:T(4,128)S(1)}, f32[2,4,512]{2,1,0:T(4,128)S(1)}, u32[]{:S(2)}, u32[]{:S(2)}) collective-permute-start(f32[2,4,512]{2,1,0:T(4,128)S(1)} %pad_maximum_fusion.21), channel_id=1, source_target_pairs={{15,0},{0,1},{1,2},{2,3},{3,4},{4,5},{5,6},{6,7},{7,8},{8,9},{9,10... | collective-permute-start | bytes 49160 | tf_op jit(solution)/shard_map/ppermute | solution.py:13
  65.5 53.2 %collective-permute-start.5 = (f32[4,128,512]{2,1,0:T(8,128)S(1)}, f32[4,128,512]{2,1,0:T(8,128)S(1)}, u32[]{:S(2)}, u32[]{:S(2)}) collective-permute-start(f32[4,128,512]{2,1,0:T(8,128)S(1)} %pad_maximum_fusion.5), channel_id=1, source_target_pairs={{240,0},{0,16},{16,32},{32,48},{48,64},{64,80},{80,96},{96,112},{1... | collective-permute-start | bytes 3145736 | tf_op jit(solution)/shard_map/ppermute | solution.py:13
  70.4 48.0 %collective-permute-start.7 = (f32[4,128,512]{2,1,0:T(8,128)S(1)}, f32[4,128,512]{2,1,0:T(8,128)S(1)}, u32[]{:S(2)}, u32[]{:S(2)}) collective-permute-start(f32[4,128,512]{2,1,0:T(8,128)S(1)} %pad_maximum_fusion.4), channel_id=1, source_target_pairs={{16,0},{32,16},{48,32},{64,48},{80,64},{96,80},{112,96},{128,112},... | collective-permute-start | bytes 3145736 | tf_op jit(solution)/shard_map/ppermute | solution.py:13
  119.4 5.6 %collective-permute-start.6 = (f32[2,4,512]{2,1,0:T(4,128)S(1)}, f32[2,4,512]{2,1,0:T(4,128)S(1)}, u32[]{:S(2)}, u32[]{:S(2)}) collective-permute-start(f32[2,4,512]{2,1,0:T(4,128)S(1)} %pad_maximum_fusion.22), channel_id=1, source_target_pairs={{1,0},{2,1},{3,2},{4,3},{5,4},{6,5},{7,6},{8,7},{9,8},{10,9},{11,1... | collective-permute-start | bytes 49160 | tf_op jit(solution)/shard_map/ppermute | solution.py:13
where the time goes:
time: 133 us; the launch traced here: 132 us
  waiting for transfers between devices  80.1 us (60%)
  starting transfers between devices  23.3 us (18%)
  other arithmetic  16.7 us (13%)
  local copies, waits for them, and re-layouts  10.6 us (8%)
  between operations  1.69 us (1%)
    ppermute x8, waiting for transfers between devices, from_behind(): return lax.ppermute(block, axis, route)  80.1 us
    ppermute x8, starting transfers between devices, from_behind(): return lax.ppermute(block, axis, route)  23.3 us
    unnamed x17, local copies, waits for them, and re-layouts  6.48 us
    another operation x10, other arithmetic, electric_plane(): jnp.stack([e[0] - TIME_STEP * (ahead_y(h[2], rows[1]) - ahead_z(h[1])) +...  3.03 us
  transfers between devices with their start and end apart: 8, of which 4 were waited for; matrix products, arithmetic and copies ran while one was open for 6% of the time, Pallas kernels for 0%

commit v1 on v0

--- a/solution.py
+++ b/solution.py
@@ -113,10 +113,8 @@
       hs_new[0] = jnp.stack(
           [hs_new[0][0], hs_new[0][1] + TIME_STEP * before_x[3], hs_new[0][2] - TIME_STEP * before_x[2]]
       )
-      ha, hs = ha_new, hs_new
-      front_y = jnp.stack(
-          [jnp.stack([ha[p][0, 0], ha[p][2, 0], hs[p][0, 0], hs[p][2, 0]]) for p in range(planes)]
-      )
+      ha, hs = lax.optimization_barrier((ha_new, hs_new))
+      front_y = jnp.stack([jnp.stack([ha[p][0, 0], ha[p][2, 0], hs[p][0, 0], hs[p][2, 0]]) for p in range(planes)])
       after_y = from_behind(front_y, "gy", -1)
       right_a = jnp.stack([after_x[0] + TIME_STEP * edge_x[1], after_x[1] - TIME_STEP * edge_x[0]])
       right_s = jnp.stack([after_x[2] + TIME_STEP * edge_x[3], after_x[3] - TIME_STEP * edge_x[2]])

time: 133 us -> 128 us (0.962)
  the two profiles are of different devices: /device:TPU:25 before, /device:TPU:157 now
where the time goes in v1:
time: 128 us
  waiting for transfers between devices  89.9 us (70%)
  other arithmetic  17.1 us (13%)
  local copies, waits for them, and re-layouts  10.5 us (8%)
  starting transfers between devices  8.89 us (7%)
  between operations  1.62 us (1%)
    ppermute x8, waiting for transfers between devices, from_behind(): return lax.ppermute(block, axis, route)  89.9 us
    ppermute x8, starting transfers between devices, from_behind(): return lax.ppermute(block, axis, route)  8.89 us
    unnamed x17, local copies, waits for them, and re-layouts  6.79 us
  transfers between devices with their start and end apart: 8, of which 5 were waited for; matrix products, arithmetic and copies ran while one was open for 7% of the time, Pallas kernels for 0%

profile of v1, /device:TPU:157, one launch (start us, length us, event | category | flops | bytes accessed | tf_op | source)
XLA Modules:
  0.0 128.0 jit_solution(18070482185301127090)
XLA Ops:
  0.6 1.3 %multiply_divide_fusion.1 = (f32[2,128,512]{2,1,0:T(8,128)S(1)}, pred[2,128,512]{2,1,0:T(8,128)(4,1)S(1)}, pred[2,128,512]{2,1,0:T(8,128)(4,1)S(1)}) fusion(s32[2,128,512]{2,1,0:T(8,128)} %param.16), kind=kLoop, calls=%fused_computation.74 | loop fusion | flops 786432 | bytes 1310720 | tf_op jit(solution)/shard_map/div | solution.py:74
  2.4 1.0 copy-done.1
  3.4 0.5 copy-done
  3.9 0.5 fusion.13
  4.6 1.2 collective-permute-start
  6.0 1.1 collective-permute-start.1
  7.3 1.3 copy-done.2
  8.7 1.3 copy-done.3
  10.4 0.9 convert_multiply_fusion.5
  12.6 1.0 copy-done.5
  14.6 2.1 %collective-permute-start.3 = (f32[4,128,512]{2,1,0:T(8,128)S(1)}, f32[4,128,512]{2,1,0:T(8,128)S(1)}, u32[]{:S(2)}, u32[]{:S(2)}) collective-permute-start(f32[4,128,512]{2,1,0:T(8,128)S(1)} %pad_maximum_fusion.2), channel_id=1, source_target_pairs={{16,0},{32,16},{48,32},{64,48},{80,64},{96,80},{112,96},{128,112},... | collective-permute-start | bytes 3145736 | tf_op jit(solution)/shard_map/ppermute | solution.py:13
  16.8 38.4 %collective-permute-done.1 = f32[4,128,512]{2,1,0:T(8,128)S(1)} collective-permute-done((f32[4,128,512]{2,1,0:T(8,128)S(1)}, f32[4,128,512]{2,1,0:T(8,128)S(1)}, u32[]{:S(2)}, u32[]{:S(2)}) %collective-permute-start.1) | collective-permute-done | bytes 1048608 | tf_op jit(solution)/shard_map/ppermute | solution.py:13
  55.8 0.7 collective-permute-start.2
  56.6 4.7 %collective-permute-done.2 = f32[2,4,512]{2,1,0:T(4,128)S(1)} collective-permute-done((f32[2,4,512]{2,1,0:T(4,128)S(1)}, f32[2,4,512]{2,1,0:T(4,128)S(1)}, u32[]{:S(2)}, u32[]{:S(2)}) %collective-permute-start.2) | collective-permute-done | bytes 16416 | tf_op jit(solution)/shard_map/ppermute | solution.py:13
  61.3 0.4 slice_add_fusion.8
  62.0 0.4 slice_add_fusion.10
  64.3 0.4 fusion.77
  64.7 0.4 fusion.66
  65.0 0.6 fusion.1
  66.5 1.0 collective-permute-done.4
  68.7 2.1 %collective-permute-start.7 = (f32[4,128,512]{2,1,0:T(8,128)S(1)}, f32[4,128,512]{2,1,0:T(8,128)S(1)}, u32[]{:S(2)}, u32[]{:S(2)}) collective-permute-start(f32[4,128,512]{2,1,0:T(8,128)S(1)} %pad_maximum_fusion.4), channel_id=1, source_target_pairs={{16,0},{32,16},{48,32},{64,48},{80,64},{96,80},{112,96},{128,112},... | collective-permute-start | bytes 3145736 | tf_op jit(solution)/shard_map/ppermute | solution.py:13
  71.5 43.2 %collective-permute-done.5 = f32[4,128,512]{2,1,0:T(8,128)S(1)} collective-permute-done((f32[4,128,512]{2,1,0:T(8,128)S(1)}, f32[4,128,512]{2,1,0:T(8,128)S(1)}, u32[]{:S(2)}, u32[]{:S(2)}) %collective-permute-start.5) | collective-permute-done | bytes 1048608 | tf_op jit(solution)/shard_map/ppermute | solution.py:13
  115.4 1.6 %collective-permute-start.6 = (f32[2,4,512]{2,1,0:T(4,128)S(1)}, f32[2,4,512]{2,1,0:T(4,128)S(1)}, u32[]{:S(2)}, u32[]{:S(2)}) collective-permute-start(f32[2,4,512]{2,1,0:T(4,128)S(1)} %pad_maximum_fusion.30), channel_id=1, source_target_pairs={{1,0},{2,1},{3,2},{4,3},{5,4},{6,5},{7,6},{8,7},{9,8},{10,9},{11,1... | collective-permute-start | bytes 49160 | tf_op jit(solution)/shard_map/ppermute | solution.py:13
  117.1 1.3 pad_maximum_fusion.1
  118.3 2.6 %collective-permute-done.6 = f32[2,4,512]{2,1,0:T(4,128)S(1)} collective-permute-done((f32[2,4,512]{2,1,0:T(4,128)S(1)}, f32[2,4,512]{2,1,0:T(4,128)S(1)}, u32[]{:S(2)}, u32[]{:S(2)}) %collective-permute-start.6) | collective-permute-done | bytes 16416 | tf_op jit(solution)/shard_map/ppermute | solution.py:13
  122.0 0.4 slice_add_fusion
  122.9 0.4 fusion.30
  124.1 0.4 fusion.43
  124.8 0.6 fusion.3
  125.6 1.3 copy.21
  126.8 0.4 fusion.182
  127.2 0.8 pad_maximum_fusion.26
  (133 shorter events, 12.2 us)
Async XLA Ops:
  0.6 1.3 %copy-start.7 = (f32[2,128,512]{2,1,0:T(8,128)S(1)}, f32[2,128,512]{2,1,0:T(8,128)}, u32[]{:S(2)}) copy-start(f32[2,128,512]{2,1,0:T(8,128)} %param.15) | copy-start | bytes 1572868
  2.0 1.4 %copy-start.1 = (f32[3,2,128,512]{3,2,1,0:T(8,128)S(1)}, f32[3,2,128,512]{3,2,1,0:T(8,128)}, u32[]{:S(2)}) copy-start(f32[3,2,128,512]{3,2,1,0:T(8,128)} %param.11) | copy-start | bytes 4718596
  2.3 1.7 %copy-start = (f32[3,2,128,512]{3,2,1,0:T(8,128)S(1)}, f32[3,2,128,512]{3,2,1,0:T(8,128)}, u32[]{:S(2)}) copy-start(f32[3,2,128,512]{3,2,1,0:T(8,128)} %param.9) | copy-start | bytes 4718596
  4.6 6.8 %collective-permute-start = (f32[2,4,512]{2,1,0:T(4,128)S(1)}, f32[2,4,512]{2,1,0:T(4,128)S(1)}, u32[]{:S(2)}, u32[]{:S(2)}) collective-permute-start(f32[2,4,512]{2,1,0:T(4,128)S(1)} %pad_maximum_fusion.27), channel_id=1, source_target_pairs={{15,0},{0,1},{1,2},{2,3},{3,4},{4,5},{5,6},{6,7},{7,8},{8,9},{9,10... | collective-permute-start | bytes 49160 | tf_op jit(solution)/shard_map/ppermute | solution.py:13
  5.9 1.2 copy-start.6
  6.0 49.2 %collective-permute-start.1 = (f32[4,128,512]{2,1,0:T(8,128)S(1)}, f32[4,128,512]{2,1,0:T(8,128)S(1)}, u32[]{:S(2)}, u32[]{:S(2)}) collective-permute-start(f32[4,128,512]{2,1,0:T(8,128)S(1)} %pad_maximum_fusion.3), channel_id=1, source_target_pairs={{240,0},{0,16},{16,32},{32,48},{48,64},{64,80},{80,96},{96,112},{1... | collective-permute-start | bytes 3145736 | tf_op jit(solution)/shard_map/ppermute | solution.py:13
  7.1 1.4 %copy-start.2 = (bf16[2,3,2,128,512]{4,3,2,1,0:T(8,128)(2,1)S(1)}, bf16[2,3,2,128,512]{4,3,2,1,0:T(8,128)(2,1)}, u32[]{:S(2)}) copy-start(bf16[2,3,2,128,512]{4,3,2,1,0:T(8,128)(2,1)} %param.13) | copy-start | bytes 4718596
  8.5 1.4 %copy-start.3 = (bf16[2,3,2,128,512]{4,3,2,1,0:T(8,128)(2,1)S(1)}, bf16[2,3,2,128,512]{4,3,2,1,0:T(8,128)(2,1)}, u32[]{:S(2)}) copy-start(bf16[2,3,2,128,512]{4,3,2,1,0:T(8,128)(2,1)} %param.14) | copy-start | bytes 4718596
  10.4 1.4 %copy-start.4 = (f32[3,2,128,512]{3,2,1,0:T(8,128)S(1)}, f32[3,2,128,512]{3,2,1,0:T(8,128)}, u32[]{:S(2)}) copy-start(f32[3,2,128,512]{3,2,1,0:T(8,128)} %param.10) | copy-start | bytes 4718596
  12.2 1.4 %copy-start.5 = (f32[3,2,128,512]{3,2,1,0:T(8,128)S(1)}, f32[3,2,128,512]{3,2,1,0:T(8,128)}, u32[]{:S(2)}) copy-start(f32[3,2,128,512]{3,2,1,0:T(8,128)} %param.12) | copy-start | bytes 4718596
  14.6 46.7 %collective-permute-start.3 = (f32[4,128,512]{2,1,0:T(8,128)S(1)}, f32[4,128,512]{2,1,0:T(8,128)S(1)}, u32[]{:S(2)}, u32[]{:S(2)}) collective-permute-start(f32[4,128,512]{2,1,0:T(8,128)S(1)} %pad_maximum_fusion.2), channel_id=1, source_target_pairs={{16,0},{32,16},{48,32},{64,48},{80,64},{96,80},{112,96},{128,112},... | collective-permute-start | bytes 3145736 | tf_op jit(solution)/shard_map/ppermute | solution.py:13
  55.8 5.5 %collective-permute-start.2 = (f32[2,4,512]{2,1,0:T(4,128)S(1)}, f32[2,4,512]{2,1,0:T(4,128)S(1)}, u32[]{:S(2)}, u32[]{:S(2)}) collective-permute-start(f32[2,4,512]{2,1,0:T(4,128)S(1)} %pad_maximum_fusion.28), channel_id=1, source_target_pairs={{1,0},{2,1},{3,2},{4,3},{5,4},{6,5},{7,6},{8,7},{9,8},{10,9},{11,1... | collective-permute-start | bytes 49160 | tf_op jit(solution)/shard_map/ppermute | solution.py:13
  66.2 1.3 collective-permute-start.4
  66.4 48.3 %collective-permute-start.5 = (f32[4,128,512]{2,1,0:T(8,128)S(1)}, f32[4,128,512]{2,1,0:T(8,128)S(1)}, u32[]{:S(2)}, u32[]{:S(2)}) collective-permute-start(f32[4,128,512]{2,1,0:T(8,128)S(1)} %pad_maximum_fusion.5), channel_id=1, source_target_pairs={{240,0},{0,16},{16,32},{32,48},{48,64},{64,80},{80,96},{96,112},{1... | collective-permute-start | bytes 3145736 | tf_op jit(solution)/shard_map/ppermute | solution.py:13
  68.7 53.3 %collective-permute-start.7 = (f32[4,128,512]{2,1,0:T(8,128)S(1)}, f32[4,128,512]{2,1,0:T(8,128)S(1)}, u32[]{:S(2)}, u32[]{:S(2)}) collective-permute-start(f32[4,128,512]{2,1,0:T(8,128)S(1)} %pad_maximum_fusion.4), channel_id=1, source_target_pairs={{16,0},{32,16},{48,32},{64,48},{80,64},{96,80},{112,96},{128,112},... | collective-permute-start | bytes 3145736 | tf_op jit(solution)/shard_map/ppermute | solution.py:13
  115.4 5.6 %collective-permute-start.6 = (f32[2,4,512]{2,1,0:T(4,128)S(1)}, f32[2,4,512]{2,1,0:T(4,128)S(1)}, u32[]{:S(2)}, u32[]{:S(2)}) collective-permute-start(f32[2,4,512]{2,1,0:T(4,128)S(1)} %pad_maximum_fusion.30), channel_id=1, source_target_pairs={{1,0},{2,1},{3,2},{4,3},{5,4},{6,5},{7,6},{8,7},{9,8},{10,9},{11,1... | collective-permute-start | bytes 49160 | tf_op jit(solution)/shard_map/ppermute | solution.py:13

commit v2 on v1

--- a/solution.py
+++ b/solution.py
@@ -11,6 +11,15 @@
     devices = range(lax.axis_size(axis))
     route = [((i - distance) % len(devices), i) for i in devices]
     return lax.ppermute(block, axis, route)
+
+
+def diagonal_route():
+    nx, ny = lax.axis_size("gx"), lax.axis_size("gy")
+    return [(i * ny + j, ((i - 1) % nx) * ny + (j + 1) % ny) for i in range(nx) for j in range(ny)]
+
+
+def add_row0(f, row):
+    return jnp.concatenate([(f[0] + row)[None], f[1:]], axis=0)
 
 
 def back_y(f, row):
@@ -99,25 +108,39 @@
 
       ha_new = [None] * planes
       hs_new = [None] * planes
-      ha_new[0] = magnetic_plane(ha[0], wa[0], None, before_y[0, 0:2])
-      hs_new[0] = magnetic_plane(hs[0], ws[0], None, before_y[0, 2:4])
-      front_x = jnp.stack([ha_new[0][1], ha_new[0][2], hs_new[0][1], hs_new[0][2]])
-      ha_new[0], hs_new[0], front_x = lax.optimization_barrier((ha_new[0], hs_new[0], front_x))
+      edge_d = jnp.stack([wa[0][0, -1], ws[0][0, -1]])
+      before_d = lax.ppermute(edge_d, ("gx", "gy"), diagonal_route())
+      no_rows = jnp.zeros((2,) + wa[0].shape[2:], wa[0].dtype)
+      pa = magnetic_plane(ha[0], wa[0], None, no_rows)
+      ps = magnetic_plane(hs[0], ws[0], None, no_rows)
+      front_x = lax.optimization_barrier(jnp.stack([pa[1], pa[2], ps[1], ps[2]]))
       after_x = from_behind(front_x, "gx", -1)
       for p in range(1, planes):
           ha_new[p] = magnetic_plane(ha[p], wa[p], wa[p - 1], before_y[p, 0:2])
           hs_new[p] = magnetic_plane(hs[p], ws[p], ws[p - 1], before_y[p, 2:4])
       ha_new[0] = jnp.stack(
-          [ha_new[0][0], ha_new[0][1] + TIME_STEP * before_x[1], ha_new[0][2] - TIME_STEP * before_x[0]]
+          [
+              ha[0][0] + TIME_STEP * (back_y(wa[0][2], before_y[0, 1]) - back_z(wa[0][1])),
+              front_x[0] + TIME_STEP * before_x[1],
+              add_row0(front_x[1] - TIME_STEP * before_x[0], TIME_STEP * before_y[0, 0]),
+          ]
       )
       hs_new[0] = jnp.stack(
-          [hs_new[0][0], hs_new[0][1] + TIME_STEP * before_x[3], hs_new[0][2] - TIME_STEP * before_x[2]]
+          [
+              hs[0][0] + TIME_STEP * (back_y(ws[0][2], before_y[0, 3]) - back_z(ws[0][1])),
+              front_x[2] + TIME_STEP * before_x[3],
+              add_row0(front_x[3] - TIME_STEP * before_x[2], TIME_STEP * before_y[0, 2]),
+          ]
       )
       ha, hs = lax.optimization_barrier((ha_new, hs_new))
       front_y = jnp.stack([jnp.stack([ha[p][0, 0], ha[p][2, 0], hs[p][0, 0], hs[p][2, 0]]) for p in range(planes)])
       after_y = from_behind(front_y, "gy", -1)
-      right_a = jnp.stack([after_x[0] + TIME_STEP * edge_x[1], after_x[1] - TIME_STEP * edge_x[0]])
-      right_s = jnp.stack([after_x[2] + TIME_STEP * edge_x[3], after_x[3] - TIME_STEP * edge_x[2]])
+      right_a = jnp.stack(
+          [after_x[0] + TIME_STEP * edge_x[1], add_row0(after_x[1] - TIME_STEP * edge_x[0], TIME_STEP * before_d[0])]
+      )
+      right_s = jnp.stack(
+          [after_x[2] + TIME_STEP * edge_x[3], add_row0(after_x[3] - TIME_STEP * edge_x[2], TIME_STEP * before_d[1])]
+      )
 
       ea_new = [None] * planes
       es_new = [None] * planes

time: 128 us -> 139 us (1.086)
  the two profiles are of different devices: /device:TPU:157 before, /device:TPU:25 now
where the time goes in v2:
time: 139 us
  waiting for transfers between devices  85.1 us (61%)
  starting transfers between devices  24.5 us (18%)
  other arithmetic  17 us (12%)
  local copies, waits for them, and re-layouts  10.7 us (8%)
  between operations  1.67 us (1%)
    ppermute x8, waiting for transfers between devices, from_behind(): return lax.ppermute(block, axis, route)  85.1 us
    ppermute x8, starting transfers between devices, from_behind(): return lax.ppermute(block, axis, route)  12.5 us
    ppermute x2, starting transfers between devices, local(): before_d = lax.ppermute(edge_d, ('gx', 'gy'), diagonal_route())  12 us
    unnamed x17, local copies, waits for them, and re-layouts  6.73 us
  transfers between devices with their start and end apart: 10, of which 6 were waited for; matrix products, arithmetic and copies ran while one was open for 8% of the time, Pallas kernels for 0%

profile of v2, /device:TPU:25, one launch (start us, length us, event | category | flops | bytes accessed | tf_op | source)
XLA Modules:
  0.0 138.9 jit_solution(8906065295690283250)
XLA Ops:
  0.6 1.3 multiply_divide_fusion.1
  2.4 1.0 copy-done.1
  3.4 0.5 copy-done
  3.9 0.5 fusion.13
  4.5 8.1 %collective-permute-start.4 = (f32[2,512]{1,0:T(2,128)S(1)}, f32[2,512]{1,0:T(2,128)S(1)}, u32[]{:S(2)}, u32[]{:S(2)}) collective-permute-start(f32[2,512]{1,0:T(2,128)S(1)} %pad_maximum_fusion.27), channel_id=1, source_target_pairs={{0,241},{1,242},{2,243},{3,244},{4,245},{5,246},{6,247},{7,248},{8... | collective-permute-start | bytes 12296 | tf_op jit(solution)/shard_map/ppermute | solution.py:112
  13.4 0.8 copy-done.6
  14.3 0.5 copy-done.2
  15.0 1.3 copy-done.3
  16.7 0.9 convert_multiply_fusion.5
  18.3 0.9 copy-done.4
  19.4 0.5 fusion.77
  20.1 5.1 %collective-permute-start.3 = (f32[4,128,512]{2,1,0:T(8,128)S(1)}, f32[4,128,512]{2,1,0:T(8,128)S(1)}, u32[]{:S(2)}, u32[]{:S(2)}) collective-permute-start(f32[4,128,512]{2,1,0:T(8,128)S(1)} %pad_maximum_fusion.2), channel_id=1, source_target_pairs={{16,0},{32,16},{48,32},{64,48},{80,64},{96,80},{112,96},{128,112},... | collective-permute-start | bytes 3145736 | tf_op jit(solution)/shard_map/ppermute | solution.py:13
  25.3 0.4 fusion.88
  25.9 32.4 %collective-permute-done.1 = f32[4,128,512]{2,1,0:T(8,128)S(1)} collective-permute-done((f32[4,128,512]{2,1,0:T(8,128)S(1)}, f32[4,128,512]{2,1,0:T(8,128)S(1)}, u32[]{:S(2)}, u32[]{:S(2)}) %collective-permute-start.1) | collective-permute-done | bytes 1048608 | tf_op jit(solution)/shard_map/ppermute | solution.py:13
  59.0 1.0 collective-permute-start.2
  60.2 4.3 %collective-permute-done.2 = f32[2,4,512]{2,1,0:T(4,128)S(1)} collective-permute-done((f32[2,4,512]{2,1,0:T(4,128)S(1)}, f32[2,4,512]{2,1,0:T(4,128)S(1)}, u32[]{:S(2)}, u32[]{:S(2)}) %collective-permute-start.2) | collective-permute-done | bytes 16416 | tf_op jit(solution)/shard_map/ppermute | solution.py:13
  64.6 0.4 slice_add_fusion.10
  68.4 0.6 fusion.1
  69.5 3.9 %collective-permute-start.9 = (f32[2,512]{1,0:T(2,128)S(1)}, f32[2,512]{1,0:T(2,128)S(1)}, u32[]{:S(2)}, u32[]{:S(2)}) collective-permute-start(f32[2,512]{1,0:T(2,128)S(1)} %pad_maximum_fusion.28), channel_id=1, source_target_pairs={{0,241},{1,242},{2,243},{3,244},{4,245},{5,246},{6,247},{7,248},{8... | collective-permute-start | bytes 12296 | tf_op jit(solution)/shard_map/ppermute | solution.py:112
  73.5 0.8 collective-permute-start.5
  74.4 0.5 collective-permute-start.6
  75.0 0.9 collective-permute-done.5
  76.9 3.8 %collective-permute-start.8 = (f32[4,128,512]{2,1,0:T(8,128)S(1)}, f32[4,128,512]{2,1,0:T(8,128)S(1)}, u32[]{:S(2)}, u32[]{:S(2)}) collective-permute-start(f32[4,128,512]{2,1,0:T(8,128)S(1)} %pad_maximum_fusion.4), channel_id=1, source_target_pairs={{16,0},{32,16},{48,32},{64,48},{80,64},{96,80},{112,96},{128,112},... | collective-permute-start | bytes 3145736 | tf_op jit(solution)/shard_map/ppermute | solution.py:13
  81.1 38.7 %collective-permute-done.6 = f32[4,128,512]{2,1,0:T(8,128)S(1)} collective-permute-done((f32[4,128,512]{2,1,0:T(8,128)S(1)}, f32[4,128,512]{2,1,0:T(8,128)S(1)}, u32[]{:S(2)}, u32[]{:S(2)}) %collective-permute-start.6) | collective-permute-done | bytes 1048608 | tf_op jit(solution)/shard_map/ppermute | solution.py:13
  120.3 5.3 %collective-permute-done.8 = f32[4,128,512]{2,1,0:T(8,128)S(1)} collective-permute-done((f32[4,128,512]{2,1,0:T(8,128)S(1)}, f32[4,128,512]{2,1,0:T(8,128)S(1)}, u32[]{:S(2)}, u32[]{:S(2)}) %collective-permute-start.8) | collective-permute-done | bytes 1048608 | tf_op jit(solution)/shard_map/ppermute | solution.py:13
  126.4 0.8 collective-permute-start.7
  127.2 1.3 pad_maximum_fusion.1
  128.6 3.4 %collective-permute-done.7 = f32[2,4,512]{2,1,0:T(4,128)S(1)} collective-permute-done((f32[2,4,512]{2,1,0:T(4,128)S(1)}, f32[2,4,512]{2,1,0:T(4,128)S(1)}, u32[]{:S(2)}, u32[]{:S(2)}) %collective-permute-start.7) | collective-permute-done | bytes 16416 | tf_op jit(solution)/shard_map/ppermute | solution.py:13
  132.5 0.4 slice_add_fusion
  135.7 0.6 fusion.3
  136.5 1.3 copy.21
  138.1 0.8 pad_maximum_fusion.22
  (152 shorter events, 13.8 us)
Async XLA Ops:
  0.6 1.3 copy-start.7
  2.0 1.4 %copy-start.1 = (f32[3,2,128,512]{3,2,1,0:T(8,128)S(1)}, f32[3,2,128,512]{3,2,1,0:T(8,128)}, u32[]{:S(2)}) copy-start(f32[3,2,128,512]{3,2,1,0:T(8,128)} %param.11) | copy-start | bytes 4718596
  2.3 1.7 %copy-start = (f32[3,2,128,512]{3,2,1,0:T(8,128)S(1)}, f32[3,2,128,512]{3,2,1,0:T(8,128)}, u32[]{:S(2)}) copy-start(f32[3,2,128,512]{3,2,1,0:T(8,128)} %param.9) | copy-start | bytes 4718596
  4.5 63.2 %collective-permute-start.4 = (f32[2,512]{1,0:T(2,128)S(1)}, f32[2,512]{1,0:T(2,128)S(1)}, u32[]{:S(2)}, u32[]{:S(2)}) collective-permute-start(f32[2,512]{1,0:T(2,128)S(1)} %pad_maximum_fusion.27), channel_id=1, source_target_pairs={{0,241},{1,242},{2,243},{3,244},{4,245},{5,246},{6,247},{7,248},{8... | collective-permute-start | bytes 12296 | tf_op jit(solution)/shard_map/ppermute | solution.py:112
  12.6 5.0 %collective-permute-start = (f32[2,4,512]{2,1,0:T(4,128)S(1)}, f32[2,4,512]{2,1,0:T(4,128)S(1)}, u32[]{:S(2)}, u32[]{:S(2)}) collective-permute-start(f32[2,4,512]{2,1,0:T(4,128)S(1)} %pad_maximum_fusion.23), channel_id=1, source_target_pairs={{15,0},{0,1},{1,2},{2,3},{3,4},{4,5},{5,6},{6,7},{7,8},{8,9},{9,10... | collective-permute-start | bytes 49160 | tf_op jit(solution)/shard_map/ppermute | solution.py:13
  13.2 1.0 copy-start.6
  13.2 45.1 %collective-permute-start.1 = (f32[4,128,512]{2,1,0:T(8,128)S(1)}, f32[4,128,512]{2,1,0:T(8,128)S(1)}, u32[]{:S(2)}, u32[]{:S(2)}) collective-permute-start(f32[4,128,512]{2,1,0:T(8,128)S(1)} %pad_maximum_fusion.3), channel_id=1, source_target_pairs={{240,0},{0,16},{16,32},{32,48},{48,64},{64,80},{80,96},{96,112},{1... | collective-permute-start | bytes 3145736 | tf_op jit(solution)/shard_map/ppermute | solution.py:13
  13.4 1.4 %copy-start.2 = (bf16[2,3,2,128,512]{4,3,2,1,0:T(8,128)(2,1)S(1)}, bf16[2,3,2,128,512]{4,3,2,1,0:T(8,128)(2,1)}, u32[]{:S(2)}) copy-start(bf16[2,3,2,128,512]{4,3,2,1,0:T(8,128)(2,1)} %param.13) | copy-start | bytes 4718596
  14.8 1.4 %copy-start.3 = (bf16[2,3,2,128,512]{4,3,2,1,0:T(8,128)(2,1)S(1)}, bf16[2,3,2,128,512]{4,3,2,1,0:T(8,128)(2,1)}, u32[]{:S(2)}) copy-start(bf16[2,3,2,128,512]{4,3,2,1,0:T(8,128)(2,1)} %param.14) | copy-start | bytes 4718596
  16.7 1.4 %copy-start.5 = (f32[3,2,128,512]{3,2,1,0:T(8,128)S(1)}, f32[3,2,128,512]{3,2,1,0:T(8,128)}, u32[]{:S(2)}) copy-start(f32[3,2,128,512]{3,2,1,0:T(8,128)} %param.10) | copy-start | bytes 4718596
  17.7 1.5 %copy-start.4 = (f32[3,2,128,512]{3,2,1,0:T(8,128)S(1)}, f32[3,2,128,512]{3,2,1,0:T(8,128)}, u32[]{:S(2)}) copy-start(f32[3,2,128,512]{3,2,1,0:T(8,128)} %param.12) | copy-start | bytes 4718596
  20.1 44.4 %collective-permute-start.3 = (f32[4,128,512]{2,1,0:T(8,128)S(1)}, f32[4,128,512]{2,1,0:T(8,128)S(1)}, u32[]{:S(2)}, u32[]{:S(2)}) collective-permute-start(f32[4,128,512]{2,1,0:T(8,128)S(1)} %pad_maximum_fusion.2), channel_id=1, source_target_pairs={{16,0},{32,16},{48,32},{64,48},{80,64},{96,80},{112,96},{128,112},... | collective-permute-start | bytes 3145736 | tf_op jit(solution)/shard_map/ppermute | solution.py:13
  59.0 5.5 %collective-permute-start.2 = (f32[2,4,512]{2,1,0:T(4,128)S(1)}, f32[2,4,512]{2,1,0:T(4,128)S(1)}, u32[]{:S(2)}, u32[]{:S(2)}) collective-permute-start(f32[2,4,512]{2,1,0:T(4,128)S(1)} %pad_maximum_fusion.24), channel_id=1, source_target_pairs={{1,0},{2,1},{3,2},{4,3},{5,4},{6,5},{7,6},{8,7},{9,8},{10,9},{11,1... | collective-permute-start | bytes 49160 | tf_op jit(solution)/shard_map/ppermute | solution.py:13
  69.5 57.7 %collective-permute-start.9 = (f32[2,512]{1,0:T(2,128)S(1)}, f32[2,512]{1,0:T(2,128)S(1)}, u32[]{:S(2)}, u32[]{:S(2)}) collective-permute-start(f32[2,512]{1,0:T(2,128)S(1)} %pad_maximum_fusion.28), channel_id=1, source_target_pairs={{0,241},{1,242},{2,243},{3,244},{4,245},{5,246},{6,247},{7,248},{8... | collective-permute-start | bytes 12296 | tf_op jit(solution)/shard_map/ppermute | solution.py:112
  73.5 2.3 %collective-permute-start.5 = (f32[2,4,512]{2,1,0:T(4,128)S(1)}, f32[2,4,512]{2,1,0:T(4,128)S(1)}, u32[]{:S(2)}, u32[]{:S(2)}) collective-permute-start(f32[2,4,512]{2,1,0:T(4,128)S(1)} %pad_maximum_fusion.25), channel_id=1, source_target_pairs={{15,0},{0,1},{1,2},{2,3},{3,4},{4,5},{5,6},{6,7},{7,8},{8,9},{9,10... | collective-permute-start | bytes 49160 | tf_op jit(solution)/shard_map/ppermute | solution.py:13
  74.4 45.4 %collective-permute-start.6 = (f32[4,128,512]{2,1,0:T(8,128)S(1)}, f32[4,128,512]{2,1,0:T(8,128)S(1)}, u32[]{:S(2)}, u32[]{:S(2)}) collective-permute-start(f32[4,128,512]{2,1,0:T(8,128)S(1)} %pad_maximum_fusion.5), channel_id=1, source_target_pairs={{240,0},{0,16},{16,32},{32,48},{48,64},{64,80},{80,96},{96,112},{1... | collective-permute-start | bytes 3145736 | tf_op jit(solution)/shard_map/ppermute | solution.py:13
  76.9 48.7 %collective-permute-start.8 = (f32[4,128,512]{2,1,0:T(8,128)S(1)}, f32[4,128,512]{2,1,0:T(8,128)S(1)}, u32[]{:S(2)}, u32[]{:S(2)}) collective-permute-start(f32[4,128,512]{2,1,0:T(8,128)S(1)} %pad_maximum_fusion.4), channel_id=1, source_target_pairs={{16,0},{32,16},{48,32},{64,48},{80,64},{96,80},{112,96},{128,112},... | collective-permute-start | bytes 3145736 | tf_op jit(solution)/shard_map/ppermute | solution.py:13
  126.4 5.6 %collective-permute-start.7 = (f32[2,4,512]{2,1,0:T(4,128)S(1)}, f32[2,4,512]{2,1,0:T(4,128)S(1)}, u32[]{:S(2)}, u32[]{:S(2)}) collective-permute-start(f32[2,4,512]{2,1,0:T(4,128)S(1)} %pad_maximum_fusion.26), channel_id=1, source_target_pairs={{1,0},{2,1},{3,2},{4,3},{5,4},{6,5},{7,6},{8,7},{9,8},{10,9},{11,1... | collective-permute-start | bytes 49160 | tf_op jit(solution)/shard_map/ppermute | solution.py:13

commit v3 on v1

--- a/solution.py
+++ b/solution.py
@@ -126,12 +126,11 @@
           nxt_s = right_s if p == last else hs[p + 1][1:3]
           ea_new[p] = electric_plane(ea[p], ha[p], nxt_a, after_y[p, 0:2], src[p] * forward[p])
           es_new[p] = electric_plane(es[p], hs[p], nxt_s, after_y[p, 2:4], src[p] * tangent[p])
+          term = -fw1[p] * jnp.sum(tangent[p] * ea_new[p] + forward[p] * es_new[p], axis=0) + fw2[
+              p
+          ] * jnp.sum(forward[p] * ea_new[p], axis=0)
+          curvature[p] = term if curvature[p] is None else curvature[p] + term
       ea, es = ea_new, es_new
-      for p in range(planes):
-          term = -fw1[p] * jnp.sum(tangent[p] * ea[p] + forward[p] * es[p], axis=0) + fw2[p] * jnp.sum(
-              forward[p] * ea[p], axis=0
-          )
-          curvature[p] = term if curvature[p] is None else curvature[p] + term
     return (
         jnp.stack(curvature),
         jnp.stack(es, axis=1),

time: 128 us -> 128 us (level)
  no operation moved by 1% of the time
where the time goes in v3:
time: 128 us
  waiting for transfers between devices  89.9 us (70%)
  other arithmetic  17.1 us (13%)
  local copies, waits for them, and re-layouts  10.5 us (8%)
  starting transfers between devices  8.89 us (7%)
  between operations  1.62 us (1%)
    ppermute x8, waiting for transfers between devices, from_behind(): return lax.ppermute(block, axis, route)  89.9 us
    ppermute x8, starting transfers between devices, from_behind(): return lax.ppermute(block, axis, route)  8.89 us
    unnamed x17, local copies, waits for them, and re-layouts  6.79 us
  transfers between devices with their start and end apart: 8, of which 5 were waited for; matrix products, arithmetic and copies ran while one was open for 7% of the time, Pallas kernels for 0%

profile of v3, /device:TPU:157, one launch (start us, length us, event | category | flops | bytes accessed | tf_op | source)
XLA Modules:
  0.0 128.0 jit_solution(18070482185301127090)
XLA Ops:
  0.6 1.3 %multiply_divide_fusion.1 = (f32[2,128,512]{2,1,0:T(8,128)S(1)}, pred[2,128,512]{2,1,0:T(8,128)(4,1)S(1)}, pred[2,128,512]{2,1,0:T(8,128)(4,1)S(1)}) fusion(s32[2,128,512]{2,1,0:T(8,128)} %param.16), kind=kLoop, calls=%fused_computation.74 | loop fusion | flops 786432 | bytes 1310720 | tf_op jit(solution)/shard_map/div | solution.py:74
  2.4 1.0 copy-done.1
  3.4 0.5 copy-done
  3.9 0.5 fusion.13
  4.6 1.2 collective-permute-start
  6.0 1.1 collective-permute-start.1
  7.3 1.3 copy-done.2
  8.7 1.3 copy-done.3
  10.4 0.9 convert_multiply_fusion.5
  12.6 1.0 copy-done.5
  14.6 2.1 %collective-permute-start.3 = (f32[4,128,512]{2,1,0:T(8,128)S(1)}, f32[4,128,512]{2,1,0:T(8,128)S(1)}, u32[]{:S(2)}, u32[]{:S(2)}) collective-permute-start(f32[4,128,512]{2,1,0:T(8,128)S(1)} %pad_maximum_fusion.2), channel_id=1, source_target_pairs={{16,0},{32,16},{48,32},{64,48},{80,64},{96,80},{112,96},{128,112},... | collective-permute-start | bytes 3145736 | tf_op jit(solution)/shard_map/ppermute | solution.py:13
  16.8 38.4 %collective-permute-done.1 = f32[4,128,512]{2,1,0:T(8,128)S(1)} collective-permute-done((f32[4,128,512]{2,1,0:T(8,128)S(1)}, f32[4,128,512]{2,1,0:T(8,128)S(1)}, u32[]{:S(2)}, u32[]{:S(2)}) %collective-permute-start.1) | collective-permute-done | bytes 1048608 | tf_op jit(solution)/shard_map/ppermute | solution.py:13
  55.8 0.7 collective-permute-start.2
  56.6 4.7 %collective-permute-done.2 = f32[2,4,512]{2,1,0:T(4,128)S(1)} collective-permute-done((f32[2,4,512]{2,1,0:T(4,128)S(1)}, f32[2,4,512]{2,1,0:T(4,128)S(1)}, u32[]{:S(2)}, u32[]{:S(2)}) %collective-permute-start.2) | collective-permute-done | bytes 16416 | tf_op jit(solution)/shard_map/ppermute | solution.py:13
  61.3 0.4 slice_add_fusion.8
  62.0 0.4 slice_add_fusion.10
  64.3 0.4 fusion.77
  64.7 0.4 fusion.66
  65.0 0.6 fusion.1
  66.5 1.0 collective-permute-done.4
  68.7 2.1 %collective-permute-start.7 = (f32[4,128,512]{2,1,0:T(8,128)S(1)}, f32[4,128,512]{2,1,0:T(8,128)S(1)}, u32[]{:S(2)}, u32[]{:S(2)}) collective-permute-start(f32[4,128,512]{2,1,0:T(8,128)S(1)} %pad_maximum_fusion.4), channel_id=1, source_target_pairs={{16,0},{32,16},{48,32},{64,48},{80,64},{96,80},{112,96},{128,112},... | collective-permute-start | bytes 3145736 | tf_op jit(solution)/shard_map/ppermute | solution.py:13
  71.5 43.2 %collective-permute-done.5 = f32[4,128,512]{2,1,0:T(8,128)S(1)} collective-permute-done((f32[4,128,512]{2,1,0:T(8,128)S(1)}, f32[4,128,512]{2,1,0:T(8,128)S(1)}, u32[]{:S(2)}, u32[]{:S(2)}) %collective-permute-start.5) | collective-permute-done | bytes 1048608 | tf_op jit(solution)/shard_map/ppermute | solution.py:13
  115.4 1.6 %collective-permute-start.6 = (f32[2,4,512]{2,1,0:T(4,128)S(1)}, f32[2,4,512]{2,1,0:T(4,128)S(1)}, u32[]{:S(2)}, u32[]{:S(2)}) collective-permute-start(f32[2,4,512]{2,1,0:T(4,128)S(1)} %pad_maximum_fusion.30), channel_id=1, source_target_pairs={{1,0},{2,1},{3,2},{4,3},{5,4},{6,5},{7,6},{8,7},{9,8},{10,9},{11,1... | collective-permute-start | bytes 49160 | tf_op jit(solution)/shard_map/ppermute | solution.py:13
  117.1 1.3 pad_maximum_fusion.1
  118.3 2.6 %collective-permute-done.6 = f32[2,4,512]{2,1,0:T(4,128)S(1)} collective-permute-done((f32[2,4,512]{2,1,0:T(4,128)S(1)}, f32[2,4,512]{2,1,0:T(4,128)S(1)}, u32[]{:S(2)}, u32[]{:S(2)}) %collective-permute-start.6) | collective-permute-done | bytes 16416 | tf_op jit(solution)/shard_map/ppermute | solution.py:13
  122.0 0.4 slice_add_fusion
  122.9 0.4 fusion.30
  124.1 0.4 fusion.43
  124.8 0.6 fusion.3
  125.6 1.3 copy.21
  126.8 0.4 fusion.182
  127.2 0.8 pad_maximum_fusion.26
  (133 shorter events, 12.2 us)
Async XLA Ops:
  0.6 1.3 %copy-start.7 = (f32[2,128,512]{2,1,0:T(8,128)S(1)}, f32[2,128,512]{2,1,0:T(8,128)}, u32[]{:S(2)}) copy-start(f32[2,128,512]{2,1,0:T(8,128)} %param.15) | copy-start | bytes 1572868
  2.0 1.4 %copy-start.1 = (f32[3,2,128,512]{3,2,1,0:T(8,128)S(1)}, f32[3,2,128,512]{3,2,1,0:T(8,128)}, u32[]{:S(2)}) copy-start(f32[3,2,128,512]{3,2,1,0:T(8,128)} %param.11) | copy-start | bytes 4718596
  2.3 1.7 %copy-start = (f32[3,2,128,512]{3,2,1,0:T(8,128)S(1)}, f32[3,2,128,512]{3,2,1,0:T(8,128)}, u32[]{:S(2)}) copy-start(f32[3,2,128,512]{3,2,1,0:T(8,128)} %param.9) | copy-start | bytes 4718596
  4.6 6.8 %collective-permute-start = (f32[2,4,512]{2,1,0:T(4,128)S(1)}, f32[2,4,512]{2,1,0:T(4,128)S(1)}, u32[]{:S(2)}, u32[]{:S(2)}) collective-permute-start(f32[2,4,512]{2,1,0:T(4,128)S(1)} %pad_maximum_fusion.27), channel_id=1, source_target_pairs={{15,0},{0,1},{1,2},{2,3},{3,4},{4,5},{5,6},{6,7},{7,8},{8,9},{9,10... | collective-permute-start | bytes 49160 | tf_op jit(solution)/shard_map/ppermute | solution.py:13
  5.9 1.2 copy-start.6
  6.0 49.2 %collective-permute-start.1 = (f32[4,128,512]{2,1,0:T(8,128)S(1)}, f32[4,128,512]{2,1,0:T(8,128)S(1)}, u32[]{:S(2)}, u32[]{:S(2)}) collective-permute-start(f32[4,128,512]{2,1,0:T(8,128)S(1)} %pad_maximum_fusion.3), channel_id=1, source_target_pairs={{240,0},{0,16},{16,32},{32,48},{48,64},{64,80},{80,96},{96,112},{1... | collective-permute-start | bytes 3145736 | tf_op jit(solution)/shard_map/ppermute | solution.py:13
  7.1 1.4 %copy-start.2 = (bf16[2,3,2,128,512]{4,3,2,1,0:T(8,128)(2,1)S(1)}, bf16[2,3,2,128,512]{4,3,2,1,0:T(8,128)(2,1)}, u32[]{:S(2)}) copy-start(bf16[2,3,2,128,512]{4,3,2,1,0:T(8,128)(2,1)} %param.13) | copy-start | bytes 4718596
  8.5 1.4 %copy-start.3 = (bf16[2,3,2,128,512]{4,3,2,1,0:T(8,128)(2,1)S(1)}, bf16[2,3,2,128,512]{4,3,2,1,0:T(8,128)(2,1)}, u32[]{:S(2)}) copy-start(bf16[2,3,2,128,512]{4,3,2,1,0:T(8,128)(2,1)} %param.14) | copy-start | bytes 4718596
  10.4 1.4 %copy-start.4 = (f32[3,2,128,512]{3,2,1,0:T(8,128)S(1)}, f32[3,2,128,512]{3,2,1,0:T(8,128)}, u32[]{:S(2)}) copy-start(f32[3,2,128,512]{3,2,1,0:T(8,128)} %param.10) | copy-start | bytes 4718596
  12.2 1.4 %copy-start.5 = (f32[3,2,128,512]{3,2,1,0:T(8,128)S(1)}, f32[3,2,128,512]{3,2,1,0:T(8,128)}, u32[]{:S(2)}) copy-start(f32[3,2,128,512]{3,2,1,0:T(8,128)} %param.12) | copy-start | bytes 4718596
  14.6 46.7 %collective-permute-start.3 = (f32[4,128,512]{2,1,0:T(8,128)S(1)}, f32[4,128,512]{2,1,0:T(8,128)S(1)}, u32[]{:S(2)}, u32[]{:S(2)}) collective-permute-start(f32[4,128,512]{2,1,0:T(8,128)S(1)} %pad_maximum_fusion.2), channel_id=1, source_target_pairs={{16,0},{32,16},{48,32},{64,48},{80,64},{96,80},{112,96},{128,112},... | collective-permute-start | bytes 3145736 | tf_op jit(solution)/shard_map/ppermute | solution.py:13
  55.8 5.5 %collective-permute-start.2 = (f32[2,4,512]{2,1,0:T(4,128)S(1)}, f32[2,4,512]{2,1,0:T(4,128)S(1)}, u32[]{:S(2)}, u32[]{:S(2)}) collective-permute-start(f32[2,4,512]{2,1,0:T(4,128)S(1)} %pad_maximum_fusion.28), channel_id=1, source_target_pairs={{1,0},{2,1},{3,2},{4,3},{5,4},{6,5},{7,6},{8,7},{9,8},{10,9},{11,1... | collective-permute-start | bytes 49160 | tf_op jit(solution)/shard_map/ppermute | solution.py:13
  66.2 1.3 collective-permute-start.4
  66.4 48.3 %collective-permute-start.5 = (f32[4,128,512]{2,1,0:T(8,128)S(1)}, f32[4,128,512]{2,1,0:T(8,128)S(1)}, u32[]{:S(2)}, u32[]{:S(2)}) collective-permute-start(f32[4,128,512]{2,1,0:T(8,128)S(1)} %pad_maximum_fusion.5), channel_id=1, source_target_pairs={{240,0},{0,16},{16,32},{32,48},{48,64},{64,80},{80,96},{96,112},{1... | collective-permute-start | bytes 3145736 | tf_op jit(solution)/shard_map/ppermute | solution.py:13
  68.7 53.3 %collective-permute-start.7 = (f32[4,128,512]{2,1,0:T(8,128)S(1)}, f32[4,128,512]{2,1,0:T(8,128)S(1)}, u32[]{:S(2)}, u32[]{:S(2)}) collective-permute-start(f32[4,128,512]{2,1,0:T(8,128)S(1)} %pad_maximum_fusion.4), channel_id=1, source_target_pairs={{16,0},{32,16},{48,32},{64,48},{80,64},{96,80},{112,96},{128,112},... | collective-permute-start | bytes 3145736 | tf_op jit(solution)/shard_map/ppermute | solution.py:13
  115.4 5.6 %collective-permute-start.6 = (f32[2,4,512]{2,1,0:T(4,128)S(1)}, f32[2,4,512]{2,1,0:T(4,128)S(1)}, u32[]{:S(2)}, u32[]{:S(2)}) collective-permute-start(f32[2,4,512]{2,1,0:T(4,128)S(1)} %pad_maximum_fusion.30), channel_id=1, source_target_pairs={{1,0},{2,1},{3,2},{4,3},{5,4},{6,5},{7,6},{8,7},{9,8},{10,9},{11,1... | collective-permute-start | bytes 49160 | tf_op jit(solution)/shard_map/ppermute | solution.py:13
